TPU v7x, 32 devices: a whole 2x2x4 slice. The times are simulated.
32 devices in a mesh: section: 2 (over x), seq: 8 (over z, y), head: 2 (over core).
Axes of the slice: x: 2, y: 2, z: 4, core: 2. Of those that a mesh axis runs over, the one named last changes fastest.
Arguments:
- bwd_input: bfloat16 [2, 1024, 3584], P('section', 'seq', 'head'), may hold values from -6 to 6
- bwd_docs: int32 [2, 1024], P('section', 'seq'), may hold values from 0 to 3, as said below
- bwd_grad: bfloat16 [2, 1024, 3584], P('section', 'seq', 'head'), may hold values from -6 to 6
- proj_weight: bfloat16 [2, 256, 3584], P('section', 'seq', 'head'), may hold values from -0.09375 to 0.09375
- step_weight: float32 [2, 3584], P('section', 'head'), may hold values from -0.75 to 0.75
- step_bias: float32 [2, 56], P('section', 'head'), may hold values from -5 to -2
- rate_log: float32 [2, 56], P('section', 'head'), may hold values from -4 to 0.5
- skip_gain: float32 [2, 56], P('section', 'head'), may hold values from 0.5 to 1.5
Outputs:
- prev_grad: bfloat16 [2, 1024, 3584], P('section', 'seq', 'head')
- grad_proj: float32 [2, 256, 3584], P('section', 'seq', 'head')
- grad_step_weight: float32 [2, 3584], P('section', 'head')
- grad_step_bias: float32 [2, 56], P('section', 'head')
- grad_rate_log: float32 [2, 56], P('section', 'head')
- grad_skip: float32 [2, 56], P('section', 'head')
Inputs may be any that keep to these rules, and one draw needn't show every extreme that they name: `bwd_docs`: document ids of each row never fall, start at 0, every id occurs, and one document of each row holds 512 tokens.
All inputs are finite; a program needn't handle non-finite values.
Results may differ from a plain program's by a relative error of at most 0.023.
Values may be sent and summed in bfloat16 or wider, within the bound.
No kernel may reach another device: no remote copies, remote signals or barrier semaphores. Data moves between devices by JAX's collectives and lax.ppermute only.
A program may use at most 64 MiB of HBM per device.

v0:
```python
import jax
import jax.numpy as jnp
from jax import lax
from jax.sharding import PartitionSpec as P

EXACT = lax.Precision.HIGHEST


def shifted(block, axis, distance):
    devices = range(lax.axis_size(axis))
    route = [(i - distance, i) for i in devices if i - distance in devices]
    return lax.ppermute(block, axis, route)


def contract(spec, left, right):
    return jnp.einsum(spec, left, right, preferred_element_type=jnp.float32)


def local_setup(values, step_weight, step_bias, rate_log):
    tokens = values.shape[0]
    raw_step = (
        jnp.einsum("thp,hp->th", values.astype(jnp.float32), step_weight, precision=EXACT)
        + step_bias[None, :]
    )
    step_size = jax.nn.softplus(raw_step)
    decay_log = -jnp.exp(rate_log)[None, :] * step_size
    row_ids = lax.broadcasted_iota(jnp.int32, (tokens, tokens), 0)
    col_ids = lax.broadcasted_iota(jnp.int32, (tokens, tokens), 1)
    triangle = (row_ids >= col_ids).astype(jnp.float32)
    cumulative = jnp.dot(triangle, decay_log, precision=EXACT)
    return (step_size, cumulative, row_ids, col_ids)


def span_summary(values, mixer, step_weight, step_bias, rate_log, docs, doc_before):
    step_size, cumulative, row_ids, col_ids = local_setup(values, step_weight, step_bias, rate_log)
    final_log = cumulative[-1]
    tail_mask = (docs == docs[-1]).astype(jnp.float32)[:, None]
    tail_weight = (
        jnp.exp(jnp.where(tail_mask > 0, final_log[None, :] - cumulative, 0.0))
        * tail_mask
        * step_size
    )
    unbroken = (docs[-1] == doc_before).astype(jnp.float32)
    carry_decay = jnp.exp(final_log) * unbroken
    half_width = mixer.shape[1] // 2
    writers = mixer[:, :half_width]
    weighted = (tail_weight[:, :, None] * writers.astype(jnp.float32)[:, None, :]).astype(
        jnp.bfloat16
    )
    span_state = contract("thn,thp->hnp", weighted, values)
    return (carry_decay, span_state)


def span_output(
    values, mixer, step_weight, step_bias, rate_log, skip_gain, docs, doc_before, incoming
):
    step_size, cumulative, row_ids, col_ids = local_setup(values, step_weight, step_bias, rate_log)
    half_width = mixer.shape[1] // 2
    writers = mixer[:, :half_width]
    readers = mixer[:, half_width:]
    affinity = jnp.dot(readers, writers.T, preferred_element_type=jnp.float32)
    same_doc = ((docs[:, None] == docs[None, :]) & (row_ids >= col_ids)).astype(jnp.float32)
    heads_first = cumulative.T
    log_gap = heads_first[:, :, None] - heads_first[:, None, :]
    mixing = (
        jnp.exp(jnp.where(same_doc[None] > 0, log_gap, 0.0))
        * same_doc[None]
        * affinity[None]
        * step_size.T[:, None, :]
    )
    mixing = mixing.astype(jnp.bfloat16)
    local_part = contract("hts,shp->thp", mixing, values)
    unbroken = (docs == doc_before).astype(jnp.float32)
    carry_scale = jnp.exp(cumulative) * unbroken[:, None]
    carried = jnp.einsum("tn,hnp->thp", readers.astype(jnp.float32), incoming, precision=EXACT)
    combined = (
        values.astype(jnp.float32) * (1.0 + skip_gain)[None, :, None]
        + local_part
        + carry_scale[:, :, None] * carried
    )
    return combined.astype(jnp.bfloat16)


def scan_rounds(decay, state, axis, forward):
    size, mine = (lax.axis_size(axis), lax.axis_index(axis))
    far_decay, far_state = (decay, state)
    near_decay = jnp.ones_like(decay)
    near_state = jnp.zeros_like(state)
    distance = 1
    while distance < size:
        got_decay, got_state = shifted(
            (far_decay, far_state.astype(jnp.bfloat16)), axis, distance if forward else -distance
        )
        got_state = got_state.astype(jnp.float32)
        near_state = near_state + near_decay[:, None] * got_state
        near_decay = near_decay * got_decay
        if distance * 2 < size:
            far_state = far_state + far_decay[:, None] * got_state
            far_decay = far_decay * got_decay
        distance *= 2
    return near_state


def shards(bwd_input, bwd_docs, bwd_grad, proj_weight, step_weight, step_bias, rate_log, skip_gain):
    tokens = bwd_input.shape[1]
    channels_here = bwd_input.shape[2]
    heads_here = step_bias.shape[1]
    head_width = channels_here // heads_here
    bwd_flat = bwd_input[0]
    bwd_values = bwd_flat.reshape(tokens, heads_here, head_width)
    weight_heads = step_weight[0].reshape(heads_here, head_width)
    bias_heads = step_bias[0]
    rate_heads = rate_log[0]
    skip_heads = skip_gain[0]
    docs_bwd = bwd_docs[0]
    doc_before = shifted(docs_bwd[-1:], "seq", 1)[0]
    full_weight = lax.all_gather(proj_weight[0], "seq", axis=0, tiled=True)
    partial_value = jnp.dot(bwd_flat, full_weight.T, preferred_element_type=jnp.float32)
    mixer_bwd = lax.psum_scatter(
        partial_value.astype(jnp.bfloat16), "head", scatter_dimension=1, tiled=True
    )
    cotangent = bwd_grad[0].reshape(tokens, heads_here, head_width)

    def summary_bwd(values_in, mixer_in, weight_in, bias_in, rate_in):
        return span_summary(values_in, mixer_in, weight_in, bias_in, rate_in, docs_bwd, doc_before)

    summary_out, summary_pull = jax.vjp(
        summary_bwd, bwd_values, mixer_bwd, weight_heads, bias_heads, rate_heads
    )
    decay_bwd, state_bwd = summary_out
    state_shape = state_bwd.shape
    state_flat = state_bwd.reshape(heads_here, -1)

    def output_bwd(values_in, mixer_in, weight_in, bias_in, rate_in, skip_in, state_in):
        return span_output(
            values_in,
            mixer_in,
            weight_in,
            bias_in,
            rate_in,
            skip_in,
            docs_bwd,
            doc_before,
            state_in,
        )

    def carried_only(state_in):
        return output_bwd(
            bwd_values, mixer_bwd, weight_heads, bias_heads, rate_heads, skip_heads, state_in
        )

    state_grad = jax.vjp(carried_only, jnp.zeros(state_shape, jnp.float32))[1](cotangent)[0]
    state_grad = state_grad.reshape(heads_here, -1)
    incoming_flat = scan_rounds(decay_bwd, state_flat, "seq", True)
    adjoint_flat = scan_rounds(decay_bwd, state_grad, "seq", False)
    incoming_bwd = incoming_flat.reshape(state_shape)
    unused, output_pull = jax.vjp(
        output_bwd,
        bwd_values,
        mixer_bwd,
        weight_heads,
        bias_heads,
        rate_heads,
        skip_heads,
        incoming_bwd,
    )
    out_grads = output_pull(cotangent)
    decay_grad = jnp.sum(adjoint_flat * incoming_flat, axis=1)
    sum_grads = summary_pull((decay_grad, adjoint_flat.reshape(state_shape)))
    mixer_grad = (out_grads[1].astype(jnp.float32) + sum_grads[1].astype(jnp.float32)).astype(
        jnp.bfloat16
    )
    mixer_full = lax.all_gather(mixer_grad, "head", axis=1, tiled=True)
    back_proj = jnp.dot(mixer_full, full_weight, preferred_element_type=jnp.float32)
    value_grad = (out_grads[0].astype(jnp.float32) + sum_grads[0].astype(jnp.float32)).reshape(
        tokens, channels_here
    ) + back_proj
    value_grad = value_grad.astype(jnp.bfloat16)
    prev_part = shifted(value_grad.reshape(1, tokens, channels_here), "section", -1)
    grad_rows = lax.psum_scatter(
        lax.dot_general(
            mixer_full, bwd_flat, (((0,), (0,)), ((), ())), preferred_element_type=jnp.float32
        ).astype(jnp.bfloat16),
        "seq",
        scatter_dimension=0,
        tiled=True,
    ).astype(jnp.float32)
    totals = lax.psum(
        (
            (out_grads[2] + sum_grads[2]).reshape(channels_here),
            out_grads[3] + sum_grads[3],
            out_grads[4] + sum_grads[4],
            out_grads[5],
        ),
        "seq",
    )
    return (
        prev_part,
        grad_rows[None],
        totals[0][None],
        totals[1][None],
        totals[2][None],
        totals[3][None],
    )


def solution(mesh):
    in_specs = (
        P("section", "seq", "head"),
        P("section", "seq"),
        P("section", "seq", "head"),
        P("section", "seq", "head"),
        P("section", "head"),
        P("section", "head"),
        P("section", "head"),
        P("section", "head"),
    )
    out_specs = (
        P("section", "seq", "head"),
        P("section", "seq", "head"),
        P("section", "head"),
        P("section", "head"),
        P("section", "head"),
        P("section", "head"),
    )
    return jax.shard_map(shards, mesh=mesh, in_specs=in_specs, out_specs=out_specs, check_vma=False)
```

profile of v0, /device:TPU:0, one launch (start us, length us, event | category | flops | bytes accessed | tf_op | source)
XLA Modules:
  0.0 210.8 jit_solution(10798965876663877636)
XLA Ops:
  7.2 1.3 slice.21
  8.5 5.4 %collective-permute-start.1 = (s32[1]{0:T(128)}, s32[1]{0:T(128)}, u32[]{:S(2)}, u32[]{:S(2)}) collective-permute-start(s32[1]{0:T(128)} %bitcast.18), channel_id=1, source_target_pairs={{0,2},{2,4},{4,6},{6,8},{8,10},{10,12},{12,14},{1,3},{3,5},{5,7},{... | collective-permute-start | bytes 20 | tf_op jit(solution)/shard_map/ppermute | solution.py:12
  13.9 32.6 %all-gather = bf16[1,256,1792]{2,1,0:T(8,128)(2,1)S(1)} all-gather(bf16[1,32,1792]{2,1,0:T(8,128)(2,1)} %param.12), channel_id=2, replica_groups=mesh['section'=2,'seq'=8,'head'=2] {'seq'}, dimensions={1}, use_global_device_ids=true | all-gather | bytes 1032192 | tf_op jit(solution)/shard_map/all_gather | solution.py:117
  46.5 0.5 convolution_convert_fusion.5
  47.0 0.7 copy.113
  48.2 0.5 fusion.102
  49.2 1.3 broadcast_compare_fusion.1
  52.8 0.5 exponential_multiply_fusion.1
  53.3 0.8 reduce-scatter.7.cloned.1.call-done
  54.1 0.7 slice_convert_fusion
  54.9 1.4 fusion.37
  56.2 1.5 reshape.210
  57.7 0.7 convert_element_type.189
  58.5 4.3 %collective-permute-start = (bf16[28,4096]{1,0:T(8,128)(2,1)}, bf16[28,4096]{1,0:T(8,128)(2,1)}, u32[]{:S(2)}, u32[]{:S(2)}) collective-permute-start(bf16[28,4096]{1,0:T(8,128)(2,1)} %convert_element_type.189), channel_id=1, source_target_pairs={{0,2},{2,4},{4,6},{6,8},{8,10},{10,12},{12,14},{1,3},{3,5},{5,7},{... | collective-permute-start | bytes 688136 | tf_op jit(solution)/shard_map/ppermute | solution.py:12
  62.8 1.6 convolution_bitcast_fusion
  64.4 2.4 %copy.93 = f32[28,64,64]{2,1,0:T(8,128)} copy(f32[28,64,64]{1,2,0:T(8,128)} %convolution_bitcast_fusion) | data formatting | bytes 917504 | tf_op jit(solution)/shard_map/transpose(jvp(tn,hnp->thp))/transpose | solution.py:75
  66.8 1.5 reshape.212
  68.3 1.3 collective-permute-start.6
  69.6 1.1 fusion.56
  70.7 4.8 %collective-permute-start.3 = (bf16[28,4096]{1,0:T(8,128)(2,1)S(1)}, bf16[28,4096]{1,0:T(8,128)(2,1)S(1)}, u32[]{:S(2)}, u32[]{:S(2)}) collective-permute-start(bf16[28,4096]{1,0:T(8,128)(2,1)S(1)} %fusion.56), channel_id=1, source_target_pairs={{0,4},{2,6},{4,8},{6,10},{8,12},{10,14},{1,5},{3,7},{5,9},{7,11},{... | collective-permute-start | bytes 688136 | tf_op jit(solution)/shard_map/ppermute | solution.py:12
  75.6 2.5 %collective-permute-start.2 = (f32[28]{0:T(128)S(1)}, f32[28]{0:T(128)S(1)}, u32[]{:S(2)}, u32[]{:S(2)}) collective-permute-start(f32[28]{0:T(128)S(1)} %copy-done.36), channel_id=1, source_target_pairs={{0,2},{2,4},{4,6},{6,8},{8,10},{10,12},{12,14},{1,3},{3,5},{5,7},{... | collective-permute-start | bytes 344 | tf_op jit(solution)/shard_map/ppermute | solution.py:12
  78.0 1.3 collective-permute-start.7
  79.4 4.5 %collective-permute-done.7 = f32[28]{0:T(128)S(1)} collective-permute-done((f32[28]{0:T(128)S(1)}, f32[28]{0:T(128)S(1)}, u32[]{:S(2)}, u32[]{:S(2)}) %collective-permute-start.7) | collective-permute-done | bytes 144 | tf_op jit(solution)/shard_map/ppermute | solution.py:12
  84.3 2.0 fusion.41
  86.4 1.4 collective-permute-start.8
  87.8 0.7 broadcast_compare_fusion
  88.5 5.5 %collective-permute-start.5 = (bf16[28,4096]{1,0:T(8,128)(2,1)}, bf16[28,4096]{1,0:T(8,128)(2,1)S(1)}, u32[]{:S(2)}, u32[]{:S(2)}) collective-permute-start(bf16[28,4096]{1,0:T(8,128)(2,1)} %get-tuple-element.40), channel_id=1, source_target_pairs={{0,8},{2,10},{4,12},{6,14},{1,9},{3,11},{5,13},{7,15},{16,24},{18,... | collective-permute-start | bytes 688136 | tf_op jit(solution)/shard_map/ppermute | solution.py:12
  94.0 0.9 collective-permute-done.8
  94.9 0.9 fusion.45
  95.8 1.3 collective-permute-start.10
  97.1 0.6 add_bitcast_fusion.1
  97.7 1.4 reshape_squeeze.10
  99.1 2.6 %fusion.25 = (f32[1792]{0:T(1024)}, f32[1,128,1792]{1,2,0:T(8,128)}) fusion(bf16[1,128,1792]{1,2,0:T(8,128)(2,1)S(1)} %copy.81, bf16[1,128,1792]{1,2,0:T(8,128)(2,1)S(1)} %copy.82, f32[128,28]{0,1:T(8,128)} %copy-done.12), kind=kLoop, calls=%fused_computation.45 | loop fusion | flops 1145088 | bytes 1856512 | tf_op jit(solution)/shard_map/transpose(jvp())/reduce_sum | solution.py:77
  101.6 1.4 reduce_sum.160
  103.0 4.0 %collective-permute-start.4 = (f32[28]{0:T(128)}, f32[28]{0:T(128)}, u32[]{:S(2)}, u32[]{:S(2)}) collective-permute-start(f32[28]{0:T(128)} %copy-done.49), channel_id=1, source_target_pairs={{0,4},{2,6},{4,8},{6,10},{8,12},{10,14},{1,5},{3,7},{5,9},{7,11},{... | collective-permute-start | bytes 344 | tf_op jit(solution)/shard_map/ppermute | solution.py:12
  107.0 1.4 reduce_sum.161
  108.3 1.3 collective-permute-start.9
  109.6 0.7 mul.342
  110.3 4.3 %collective-permute-done.9 = f32[28]{0:T(128)S(1)} collective-permute-done((f32[28]{0:T(128)}, f32[28]{0:T(128)S(1)}, u32[]{:S(2)}, u32[]{:S(2)}) %collective-permute-start.9) | collective-permute-done | bytes 144 | tf_op jit(solution)/shard_map/ppermute | solution.py:12
  114.6 0.7 mul.365
  115.3 0.8 fusion.83
  116.1 0.7 copy-done.9
  116.8 2.9 %multiply_reduce_fusion.2 = (f32[28]{0:T(128)}, bf16[28,4096]{1,0:T(8,128)(2,1)S(1)}, f32[28,4096]{1,0:T(8,128)}) fusion(bf16[28,4096]{1,0:T(8,128)(2,1)} %collective-permute-done.10, f32[28]{0:T(128)S(1)} %mul.365, bf16[28,4096]{1,0:T(8,128)(2,1)S(1)} %collective-permute-done.8, f32[28]{0:T(128)} %copy-done.46, bf16[28,4096]{1,0:T(8,128)(2,1)S(1)} %copy-done.2, ...), kind=kLoop, calls=%fused_computation.79 | loop fusion | flops 1949668 | bytes 2064944 | tf_op jit(solution)/shard_map/reduce_sum | solution.py:168
  119.7 0.5 reshape.213
  121.0 1.2 fusion.100
  122.4 2.5 %fusion.12 = (f32[28,128]{1,0:T(8,128)}, f32[28,128]{1,0:T(8,128)}, f32[28,128]{1,0:T(8,128)S(1)}, bf16[128,128]{1,0:T(8,128)(2,1)S(1)}) fusion(f32[28,128]{1,0:T(8,128)S(1)} %copy.85, f32[128,128]{1,0:T(8,128)S(1)} %copy-done.15, f32[128,128]{1,0:T(8,128)S(1)} %copy-done.17, f32[28,128]{1,0:T(8,128)S(1)} %bitcast.243, pred[128,128]{1,0:T(8,128)(4,1)S(1)} %copy-done.25, ...), kind=kOutput, calls=%fused_computation.19 | convolution fusion | flops 66491904 | bytes 1169408 | tf_op jit(solution)/shard_map/transpose(jvp(hts,shp->thp))/dot_general | solution.py:16
  125.2 1.4 reshape.211
  126.6 1.2 copy.90
  127.8 1.7 fusion.87
  129.6 0.7 fusion.27
  130.3 0.7 copy.86
  131.1 2.2 %fusion.24 = bf16[128,64]{0,1:T(8,128)(2,1)S(1)} fusion(bf16[128,64]{0,1:T(8,128)(2,1)S(1)} %convolution_convert_fusion.7, f32[128,28,64]{0,2,1:T(8,128)} %bitcast.228, f32[28,64,64]{2,1,0:T(8,128)S(1)} %reshape.211), kind=kOutput, calls=%fused_computation.44 | convolution fusion | flops 176177152 | bytes 1409024 | tf_op jit(solution)/shard_map/transpose(jvp(tn,hnp->thp))/dot_general | solution.py:75
  133.2 2.0 all_gather.7
  135.4 1.4 convolution_convert_fusion
  137.2 0.8 multiply_reduce_fusion.4
  138.4 0.9 fusion.22
  139.4 0.5 fusion.18
  140.6 1.4 collective-permute-start.11
  142.1 0.8 fusion.103
  142.9 0.8 fusion.104
  143.9 22.8 %all-reduce.4 = (f32[1,1792]{1,0:T(1,128)}, f32[1,28]{1,0:T(1,128)}, f32[1,28]{1,0:T(1,128)}, f32[1,28]{1,0:T(1,128)}) all-reduce(f32[1,1792]{1,0:T(1,128)S(1)} %broadcast_in_dim.47, f32[1,28]{1,0:T(1,128)S(1)} %get-tuple-element.50, f32[1,28]{1,0:T(1,128)S(1)} %get-tuple-element.49, ...), channel_id=1, replica_groups=mesh['section'=2,'seq'=8,'head'=2] {'seq'}, use_global_device_ids=true, to_apply=%region_11.13 | all-reduce | flops 1876 | bytes 15008 | tf_op jit(solution)/shard_map/psum | solution.py:188
  166.7 34.9 %reduce-scatter.5.cloned.1.call-done = bf16[32,1792]{1,0:T(8,128)(2,1)} async-done(((bf16[256,1792]{1,0:T(8,128)(2,1)}), bf16[32,1792]{1,0:T(8,128)(2,1)}) %reduce-scatter.5.cloned.1.call-update) | async-done | bytes 114704 | tf_op jit(solution)/shard_map/reduce_scatter | solution.py:180
  201.6 1.6 bitcast_convert_fusion
  203.2 0.8 copy.118
  (170 shorter events, 5.1 us)
Async XLA Ops:
  7.2 39.4 %copy-start = (bf16[1,128,1792]{2,1,0:T(8,128)(2,1)S(1)}, bf16[1,128,1792]{2,1,0:T(8,128)(2,1)}, u32[]{:S(2)}) copy-start(bf16[1,128,1792]{2,1,0:T(8,128)(2,1)} %param.9) | copy-start | bytes 1376260
  7.2 47.0 %reduce-scatter.7.cloned.1.call-start = ((), (), s32[]{:S(2)}) async-start(), calls=%async_computation.3 | async-start | bytes 98304
  8.5 40.6 %collective-permute-start.1 = (s32[1]{0:T(128)}, s32[1]{0:T(128)}, u32[]{:S(2)}, u32[]{:S(2)}) collective-permute-start(s32[1]{0:T(128)} %bitcast.18), channel_id=1, source_target_pairs={{0,2},{2,4},{4,6},{6,8},{8,10},{10,12},{12,14},{1,3},{3,5},{5,7},{... | collective-permute-start | bytes 20 | tf_op jit(solution)/shard_map/ppermute | solution.py:12
  47.0 1.8 copy-start.50
  47.0 1.8 copy-start.7
  47.8 153.8 %reduce-scatter.5.cloned.1.call-start = ((), (), s32[]{:S(2)}) async-start(), calls=%async_computation.2 | async-start | bytes 1032192 | tf_op jit(solution)/shard_map/reduce_scatter | solution.py:180
  48.1 3.6 %copy-start.37 = (f32[1,28]{1,0:T(1,128)S(1)}, f32[1,28]{1,0:T(1,128)}, u32[]{:S(2)}) copy-start(f32[1,28]{1,0:T(1,128)} %param.14) | copy-start | bytes 340
  48.9 7.3 %copy-start.59 = (f32[28]{0:T(128)}, f32[28]{0:T(128)S(1)}, u32[]{:S(2)}) copy-start(f32[28]{0:T(128)S(1)} %negate_bitcast_fusion) | copy-start | bytes 340
  50.4 1.7 copy-start.56
  50.5 5.8 %copy-start.28 = (pred[128]{0:T(512)(128)(4,1)}, pred[128]{0:T(512)(128)(4,1)S(1)}, u32[]{:S(2)}) copy-start(pred[128]{0:T(512)(128)(4,1)S(1)} %get-tuple-element.31) | copy-start | bytes 388
  50.5 5.7 %copy-start.31 = (f32[128]{0:T(128)}, f32[128]{0:T(128)S(1)}, u32[]{:S(2)}) copy-start(f32[128]{0:T(128)S(1)} %get-tuple-element.32) | copy-start | bytes 1540
  52.0 10.8 %copy-start.12 = (f32[128,28]{0,1:T(8,128)}, f32[128,28]{0,1:T(8,128)S(1)}, u32[]{:S(2)}) copy-start(f32[128,28]{0,1:T(8,128)S(1)} %get-tuple-element.47) | copy-start | bytes 43012
  52.2 5.6 %copy-start.40 = (f32[28]{0:T(128)}, f32[28]{0:T(128)S(1)}, u32[]{:S(2)}) copy-start(f32[28]{0:T(128)S(1)} %slice_bitcast_fusion) | copy-start | bytes 340
  56.2 6.6 %copy-start.8 = (bf16[128,128]{1,0:T(8,128)(2,1)S(1)}, bf16[128,128]{1,0:T(8,128)(2,1)}, u32[]{:S(2)}) copy-start(bf16[128,128]{1,0:T(8,128)(2,1)} %reduce-scatter.7.cloned.1.call-done) | copy-start | bytes 98308
  58.5 11.2 %collective-permute-start = (bf16[28,4096]{1,0:T(8,128)(2,1)}, bf16[28,4096]{1,0:T(8,128)(2,1)}, u32[]{:S(2)}, u32[]{:S(2)}) collective-permute-start(bf16[28,4096]{1,0:T(8,128)(2,1)} %convert_element_type.189), channel_id=1, source_target_pairs={{0,2},{2,4},{4,6},{6,8},{8,10},{10,12},{12,14},{1,3},{3,5},{5,7},{... | collective-permute-start | bytes 688136 | tf_op jit(solution)/shard_map/ppermute | solution.py:12
  68.3 7.3 %copy-start.36 = (f32[28]{0:T(128)S(1)}, f32[28]{0:T(128)}, u32[]{:S(2)}) copy-start(f32[28]{0:T(128)} %exponential_multiply_fusion.1) | copy-start | bytes 340
  68.3 15.5 %collective-permute-start.6 = (bf16[28,4096]{1,0:T(8,128)(2,1)S(1)}, bf16[28,4096]{1,0:T(8,128)(2,1)S(1)}, u32[]{:S(2)}, u32[]{:S(2)}) collective-permute-start(bf16[28,4096]{1,0:T(8,128)(2,1)S(1)} %convert_element_type.200), channel_id=1, source_target_pairs={{2,0},{4,2},{6,4},{8,6},{10,8},{12,10},{14,12},{3,1},{5,3},{7,5},{... | collective-permute-start | bytes 688136 | tf_op jit(solution)/shard_map/ppermute | solution.py:12
  70.7 13.2 %collective-permute-start.3 = (bf16[28,4096]{1,0:T(8,128)(2,1)S(1)}, bf16[28,4096]{1,0:T(8,128)(2,1)S(1)}, u32[]{:S(2)}, u32[]{:S(2)}) collective-permute-start(bf16[28,4096]{1,0:T(8,128)(2,1)S(1)} %fusion.56), channel_id=1, source_target_pairs={{0,4},{2,6},{4,8},{6,10},{8,12},{10,14},{1,5},{3,7},{5,9},{7,11},{... | collective-permute-start | bytes 688136 | tf_op jit(solution)/shard_map/ppermute | solution.py:12
  75.6 3.8 %collective-permute-start.2 = (f32[28]{0:T(128)S(1)}, f32[28]{0:T(128)S(1)}, u32[]{:S(2)}, u32[]{:S(2)}) collective-permute-start(f32[28]{0:T(128)S(1)} %copy-done.36), channel_id=1, source_target_pairs={{0,2},{2,4},{4,6},{6,8},{8,10},{10,12},{12,14},{1,3},{3,5},{5,7},{... | collective-permute-start | bytes 344 | tf_op jit(solution)/shard_map/ppermute | solution.py:12
  78.0 5.8 %collective-permute-start.7 = (f32[28]{0:T(128)S(1)}, f32[28]{0:T(128)S(1)}, u32[]{:S(2)}, u32[]{:S(2)}) collective-permute-start(f32[28]{0:T(128)S(1)} %copy-done.36), channel_id=1, source_target_pairs={{2,0},{4,2},{6,4},{8,6},{10,8},{12,10},{14,12},{3,1},{5,3},{7,5},{... | collective-permute-start | bytes 344 | tf_op jit(solution)/shard_map/ppermute | solution.py:12
  79.4 4.5 %copy-start.45 = (f32[28]{0:T(128)}, f32[28]{0:T(128)S(1)}, u32[]{:S(2)}) copy-start(f32[28]{0:T(128)S(1)} %collective-permute-done.2) | copy-start | bytes 340
  83.8 2.5 %copy-start.49 = (f32[28]{0:T(128)}, f32[28]{0:T(128)S(1)}, u32[]{:S(2)}) copy-start(f32[28]{0:T(128)S(1)} %get-tuple-element.42) | copy-start | bytes 340
  83.9 11.1 %copy-start.47 = (f32[28]{0:T(128)}, f32[28]{0:T(128)S(1)}, u32[]{:S(2)}) copy-start(f32[28]{0:T(128)S(1)} %get-tuple-element.43) | copy-start | bytes 340
  83.9 11.0 %copy-start.1 = (bf16[28,4096]{1,0:T(8,128)(2,1)}, bf16[28,4096]{1,0:T(8,128)(2,1)S(1)}, u32[]{:S(2)}) copy-start(bf16[28,4096]{1,0:T(8,128)(2,1)S(1)} %collective-permute-done.6) | copy-start | bytes 688132
  84.3 2.0 copy-start.5
  84.3 3.4 %copy-start.35 = (s32[1,128]{1,0:T(1,128)S(1)}, s32[1,128]{1,0:T(1,128)}, u32[]{:S(2)}) copy-start(s32[1,128]{1,0:T(1,128)} %param.10) | copy-start | bytes 1540
  86.4 10.7 %copy-start.58 = (f32[1,28]{1,0:T(1,128)S(1)}, f32[1,28]{1,0:T(1,128)}, u32[]{:S(2)}) copy-start(f32[1,28]{1,0:T(1,128)} %param.16) | copy-start | bytes 340
  86.4 8.6 %collective-permute-start.8 = (bf16[28,4096]{1,0:T(8,128)(2,1)S(1)}, bf16[28,4096]{1,0:T(8,128)(2,1)S(1)}, u32[]{:S(2)}, u32[]{:S(2)}) collective-permute-start(bf16[28,4096]{1,0:T(8,128)(2,1)S(1)} %get-tuple-element.41), channel_id=1, source_target_pairs={{4,0},{6,2},{8,4},{10,6},{12,8},{14,10},{5,1},{7,3},{9,5},{11,7},{... | collective-permute-start | bytes 688136 | tf_op jit(solution)/shard_map/ppermute | solution.py:12
  88.5 27.6 %collective-permute-start.5 = (bf16[28,4096]{1,0:T(8,128)(2,1)}, bf16[28,4096]{1,0:T(8,128)(2,1)S(1)}, u32[]{:S(2)}, u32[]{:S(2)}) collective-permute-start(bf16[28,4096]{1,0:T(8,128)(2,1)} %get-tuple-element.40), channel_id=1, source_target_pairs={{0,8},{2,10},{4,12},{6,14},{1,9},{3,11},{5,13},{7,15},{16,24},{18,... | collective-permute-start | bytes 688136 | tf_op jit(solution)/shard_map/ppermute | solution.py:12
  95.8 21.0 %collective-permute-start.10 = (bf16[28,4096]{1,0:T(8,128)(2,1)}, bf16[28,4096]{1,0:T(8,128)(2,1)}, u32[]{:S(2)}, u32[]{:S(2)}) collective-permute-start(bf16[28,4096]{1,0:T(8,128)(2,1)} %fusion.45), channel_id=1, source_target_pairs={{8,0},{10,2},{12,4},{14,6},{9,1},{11,3},{13,5},{15,7},{24,16},{26,... | collective-permute-start | bytes 688136 | tf_op jit(solution)/shard_map/ppermute | solution.py:12
  99.0 17.8 %copy-start.2 = (bf16[28,4096]{1,0:T(8,128)(2,1)S(1)}, bf16[28,4096]{1,0:T(8,128)(2,1)}, u32[]{:S(2)}) copy-start(bf16[28,4096]{1,0:T(8,128)(2,1)} %copy-done.1) | copy-start | bytes 688132
  99.1 17.8 %copy-start.6 = (bf16[28,4096]{1,0:T(8,128)(2,1)S(1)}, bf16[28,4096]{1,0:T(8,128)(2,1)}, u32[]{:S(2)}) copy-start(bf16[28,4096]{1,0:T(8,128)(2,1)} %copy-done.5) | copy-start | bytes 688132
  103.0 6.6 %collective-permute-start.4 = (f32[28]{0:T(128)}, f32[28]{0:T(128)}, u32[]{:S(2)}, u32[]{:S(2)}) collective-permute-start(f32[28]{0:T(128)} %copy-done.49), channel_id=1, source_target_pairs={{0,4},{2,6},{4,8},{6,10},{8,12},{10,14},{1,5},{3,7},{5,9},{7,11},{... | collective-permute-start | bytes 344 | tf_op jit(solution)/shard_map/ppermute | solution.py:12
  108.3 6.3 %collective-permute-start.9 = (f32[28]{0:T(128)}, f32[28]{0:T(128)S(1)}, u32[]{:S(2)}, u32[]{:S(2)}) collective-permute-start(f32[28]{0:T(128)} %copy-done.47), channel_id=1, source_target_pairs={{4,0},{6,2},{8,4},{10,6},{12,8},{14,10},{5,1},{7,3},{9,5},{11,7},{... | collective-permute-start | bytes 344 | tf_op jit(solution)/shard_map/ppermute | solution.py:12
  120.2 2.1 copy-start.3
  120.3 2.1 copy-start.15
  120.3 2.1 copy-start.17
  120.3 2.1 copy-start.21
  120.3 2.1 copy-start.25
  122.4 2.5 %copy-start.23 = (f32[28,128]{1,0:T(8,128)}, f32[28,128]{1,0:T(8,128)S(1)}, u32[]{:S(2)}) copy-start(f32[28,128]{1,0:T(8,128)S(1)} %copy.85) | copy-start | bytes 43012
  135.3 1.6 copy-start.10
  135.3 1.8 copy-start.14
  135.3 1.9 copy-start.19
  135.3 1.9 copy-start.22
  135.3 1.9 copy-start.30
  135.3 1.9 copy-start.33
  135.3 1.9 copy-start.39
  135.3 1.8 copy-start.42
  135.4 1.8 copy-start.57
  135.4 1.8 copy-start.60
  135.4 1.8 copy-start.62
  135.4 1.8 copy-start.63
  136.8 1.6 copy-start.16
  136.8 1.6 copy-start.18
  136.8 1.6 copy-start.24
  136.8 1.6 copy-start.26
  136.8 1.6 copy-start.61
  140.5 3.2 %copy-start.51 = (f32[1,28]{1,0:T(1,128)S(1)}, f32[1,28]{1,0:T(1,128)}, u32[]{:S(2)}) copy-start(f32[1,28]{1,0:T(1,128)} %param.15) | copy-start | bytes 340
  140.6 3.2 %copy-start.52 = (f32[28]{0:T(128)S(1)}, f32[28]{0:T(128)}, u32[]{:S(2)}) copy-start(f32[28]{0:T(128)} %get-tuple-element.16) | copy-start | bytes 340
  140.6 3.2 %copy-start.53 = (f32[28]{0:T(128)S(1)}, f32[28]{0:T(128)}, u32[]{:S(2)}) copy-start(f32[28]{0:T(128)} %get-tuple-element.17) | copy-start | bytes 340
  140.6 3.2 %copy-start.54 = (f32[28]{0:T(128)S(1)}, f32[28]{0:T(128)}, u32[]{:S(2)}) copy-start(f32[28]{0:T(128)} %get-tuple-element.35) | copy-start | bytes 340
  140.6 3.2 %copy-start.55 = (f32[28]{0:T(128)S(1)}, f32[28]{0:T(128)}, u32[]{:S(2)}) copy-start(f32[28]{0:T(128)} %get-tuple-element.37) | copy-start | bytes 340
  140.6 3.2 %copy-start.48 = (f32[28]{0:T(128)S(1)}, f32[28]{0:T(128)}, u32[]{:S(2)}) copy-start(f32[28]{0:T(128)} %reduce_sum.161) | copy-start | bytes 340
  140.6 26.1 %collective-permute-start.11 = (bf16[1,128,1792]{2,1,0:T(8,128)(2,1)S(1)}, bf16[1,128,1792]{2,1,0:T(8,128)(2,1)S(1)}, u32[]{:S(2)}, u32[]{:S(2)}) collective-permute-start(bf16[1,128,1792]{2,1,0:T(8,128)(2,1)S(1)} %fusion.1), channel_id=1, source_target_pairs={{16,0},{17,1},{18,2},{19,3},{20,4},{21,5},{22,6},{23,7},{24,8},{25... | collective-permute-start | bytes 1376264 | tf_op jit(solution)/shard_map/ppermute | solution.py:12
  (14 other events, 13.2 us)
Sparse Core Ops, SparseCore 0:
  47.9 6.1 reduce-scatter.6
  136.9 64.6 reduce-scatter.4
where the time goes:
time: 212 us; the launch traced here: 211 us
  blocking collectives  57.5 us (27%)
  waiting for transfers between devices  45.5 us (21%)
  starting transfers between devices  34.5 us (16%)
  other arithmetic  20.5 us (10%)
  local copies, waits for them, and re-layouts  18.9 us (9%)
  matrix products  17.6 us (8%)
  between operations  16.3 us (8%)
    reduce_scatter x1, waiting for transfers between devices, shards(): lax.psum_scatter(lax.dot_general(mixer_full, bwd_flat, (((0,), (0,)), (()...  34.9 us
    ppermute x12, starting transfers between devices, shifted(): return lax.ppermute(block, axis, route)  34.4 us
    all_gather x1, blocking collectives, shards(): full_weight = lax.all_gather(proj_weight[0], 'seq', axis=0, tiled=True)  32.6 us
    psum x1, blocking collectives, shards(): lax.psum(((out_grads[2] + sum_grads[2]).reshape(channels_here), out_grads...  22.8 us
    ppermute x12, waiting for transfers between devices, shifted(): return lax.ppermute(block, axis, route)  9.77 us
    dot_general x5, matrix products, contract(): return jnp.einsum(spec, left, right, preferred_element_type=jnp.float32)  5.53 us
    convert_element_type x5, other arithmetic, scan_rounds(): far_state.astype(jnp.bfloat16)  4.74 us
    unnamed x132, local copies, waits for them, and re-layouts  4.31 us
  transfers between devices with their start and end apart: 14, of which 5 were waited for; matrix products, arithmetic and copies ran while one was open for 13% of the time, Pallas kernels for 0%

commit v1 on v0

--- a/solution.py
+++ b/solution.py
@@ -4,6 +4,19 @@
 from jax.sharding import PartitionSpec as P
 
 EXACT = lax.Precision.HIGHEST
+
+
+def collect(x, axis, dim):
+    ways = lax.axis_size(axis)
+    up = [(d, (d + 1) % ways) for d in range(ways)]
+    down = [(d, (d - 1) % ways) for d in range(ways)]
+    earlier, later = ([x], [x])
+    for _ in range(ways // 2):
+        earlier.append(lax.ppermute(earlier[-1], axis, up))
+    for _ in range((ways - 1) // 2):
+        later.append(lax.ppermute(later[-1], axis, down))
+    line = jnp.concatenate([*earlier[::-1], *later[1:]], axis=dim)
+    return jnp.roll(line, (lax.axis_index(axis) - ways // 2) * x.shape[dim], axis=dim)
 
 
 def shifted(block, axis, distance):
@@ -114,7 +127,7 @@
     skip_heads = skip_gain[0]
     docs_bwd = bwd_docs[0]
     doc_before = shifted(docs_bwd[-1:], "seq", 1)[0]
-    full_weight = lax.all_gather(proj_weight[0], "seq", axis=0, tiled=True)
+    full_weight = collect(proj_weight[0], "seq", 0)
     partial_value = jnp.dot(bwd_flat, full_weight.T, preferred_element_type=jnp.float32)
     mixer_bwd = lax.psum_scatter(
         partial_value.astype(jnp.bfloat16), "head", scatter_dimension=1, tiled=True

time: 212 us -> 211 us (level)
  blocking collectives: 57.5 us -> 23 us
  starting transfers between devices: 34.5 us -> 52.3 us
  waiting for transfers between devices: 45.5 us -> 57.6 us
  local copies, waits for them, and re-layouts: 18.9 us -> 23.7 us
  other arithmetic: 20.5 us -> 17.2 us
  matrix products: 17.6 us -> 20.4 us
    all_gather x1 -> x0, blocking collectives: 32.6 us -> none  [shards(): full_weight = lax.all_gather(proj_weight[0], 'seq', axis=0, tiled=True)]
    ppermute x0 -> x7, starting transfers between devices: none -> 17.1 us  [the longest x3 12.6 us: collect(): later.append(lax.ppermute(later[-1], axis, down))]
    ppermute x0 -> x7, waiting for transfers between devices: none -> 9.68 us  [the longest x4 9.68 us: collect(): earlier.append(lax.ppermute(earlier[-1], axis, up))]
    unnamed x132 -> x104, local copies, waits for them, and re-layouts: 4.31 us -> 12.4 us
    reduce_scatter x0 -> x1, waiting for transfers between devices: none -> 5.95 us  [shards(): lax.psum_scatter(partial_value.astype(jnp.bfloat16), 'head', scatter_dime...]
    reduce_sum x2, other arithmetic: 3.95 us -> 0.97 us  [span_output(): values.astype(jnp.float32) * (1.0 + skip_gain)[None, :, None] + local_part]
    ppermute x12, waiting for transfers between devices: 9.77 us -> 7.62 us  [shifted(): return lax.ppermute(block, axis, route)]
  transfers between devices with their start and end apart: 14 -> 21, of which waited for: 5 -> 8; matrix products, arithmetic and copies ran while one was open for 13% -> 12% of each run, Pallas kernels for 0% -> 0%
where the time goes in v1:
time: 211 us; the launch traced here: 210 us
  waiting for transfers between devices  57.6 us (27%)
  starting transfers between devices  52.3 us (25%)
  local copies, waits for them, and re-layouts  23.7 us (11%)
  blocking collectives  23 us (11%)
  matrix products  20.4 us (10%)
  other arithmetic  17.2 us (8%)
  between operations  16.1 us (8%)
    ppermute x12, starting transfers between devices, shifted(): return lax.ppermute(block, axis, route)  35.1 us
    reduce_scatter x1, waiting for transfers between devices, shards(): lax.psum_scatter(lax.dot_general(mixer_full, bwd_flat, (((0,), (0,)), (()...  34.3 us
    psum x1, blocking collectives, shards(): lax.psum(((out_grads[2] + sum_grads[2]).reshape(channels_here), out_grads...  20.8 us
    ppermute x3, starting transfers between devices, collect(): later.append(lax.ppermute(later[-1], axis, down))  12.6 us
    unnamed x104, local copies, waits for them, and re-layouts  12.4 us
    ppermute x4, waiting for transfers between devices, collect(): earlier.append(lax.ppermute(earlier[-1], axis, up))  9.68 us
    ppermute x12, waiting for transfers between devices, shifted(): return lax.ppermute(block, axis, route)  7.62 us
    dot_general x5, matrix products, contract(): return jnp.einsum(spec, left, right, preferred_element_type=jnp.float32)  7.11 us
  transfers between devices with their start and end apart: 21, of which 8 were waited for; matrix products, arithmetic and copies ran while one was open for 12% of the time, Pallas kernels for 0%

profile of v1, /device:TPU:0, one launch (start us, length us, event | category | flops | bytes accessed | tf_op | source)
XLA Modules:
  0.0 210.3 jit_solution(16732169567604903135)
XLA Ops:
  7.2 3.0 %collective-permute-start = (bf16[32,1792]{1,0:T(8,128)(2,1)}, bf16[32,1792]{1,0:T(8,128)(2,1)S(1)}, u32[]{:S(2)}, u32[]{:S(2)}) collective-permute-start(bf16[32,1792]{1,0:T(8,128)(2,1)} %bitcast.230), channel_id=1, source_target_pairs={{0,2},{2,4},{4,6},{6,8},{8,10},{10,12},{12,14},{14,0},{1,3},{3,5},... | collective-permute-start | bytes 344072 | tf_op jit(solution)/shard_map/ppermute | solution.py:15
  10.3 3.1 %collective-permute-start.4 = (bf16[32,1792]{1,0:T(8,128)(2,1)}, bf16[32,1792]{1,0:T(8,128)(2,1)S(1)}, u32[]{:S(2)}, u32[]{:S(2)}) collective-permute-start(bf16[32,1792]{1,0:T(8,128)(2,1)} %bitcast.231), channel_id=1, source_target_pairs={{0,14},{2,0},{4,2},{6,4},{8,6},{10,8},{12,10},{14,12},{1,15},{3,1}... | collective-permute-start | bytes 344072 | tf_op jit(solution)/shard_map/ppermute | solution.py:17
  13.4 1.2 slice.21
  14.6 1.9 collective-permute-start.8
  16.5 1.3 copy.62
  17.8 0.7 reduce.2
  19.2 0.7 negate_bitcast_fusion
  20.1 1.3 broadcast_compare_fusion.1
  21.5 1.5 collective-permute-start.1
  23.3 5.7 %collective-permute-done.1 = bf16[32,1792]{1,0:T(8,128)(2,1)S(1)} collective-permute-done((bf16[32,1792]{1,0:T(8,128)(2,1)S(1)}, bf16[32,1792]{1,0:T(8,128)(2,1)S(1)}, u32[]{:S(2)}, u32[]{:S(2)}) %collective-permute-start.1) | collective-permute-done | bytes 114720 | tf_op jit(solution)/shard_map/ppermute | solution.py:15
  29.0 4.8 %collective-permute-start.5 = (bf16[32,1792]{1,0:T(8,128)(2,1)S(1)}, bf16[32,1792]{1,0:T(8,128)(2,1)S(1)}, u32[]{:S(2)}, u32[]{:S(2)}) collective-permute-start(bf16[32,1792]{1,0:T(8,128)(2,1)S(1)} %collective-permute-done.4), channel_id=1, source_target_pairs={{0,14},{2,0},{4,2},{6,4},{8,6},{10,8},{12,10},{14,12},{1,15},{3,1}... | collective-permute-start | bytes 344072 | tf_op jit(solution)/shard_map/ppermute | solution.py:17
  33.8 2.7 %collective-permute-done.2 = bf16[32,1792]{1,0:T(8,128)(2,1)S(1)} collective-permute-done((bf16[32,1792]{1,0:T(8,128)(2,1)S(1)}, bf16[32,1792]{1,0:T(8,128)(2,1)S(1)}, u32[]{:S(2)}, u32[]{:S(2)}) %collective-permute-start.2) | collective-permute-done | bytes 114720 | tf_op jit(solution)/shard_map/ppermute | solution.py:15
  38.0 4.8 %collective-permute-start.6 = (bf16[32,1792]{1,0:T(8,128)(2,1)S(1)}, bf16[32,1792]{1,0:T(8,128)(2,1)S(1)}, u32[]{:S(2)}, u32[]{:S(2)}) collective-permute-start(bf16[32,1792]{1,0:T(8,128)(2,1)S(1)} %collective-permute-done.5), channel_id=1, source_target_pairs={{0,14},{2,0},{4,2},{6,4},{8,6},{10,8},{12,10},{14,12},{1,15},{3,1}... | collective-permute-start | bytes 344072 | tf_op jit(solution)/shard_map/ppermute | solution.py:17
  42.8 1.3 collective-permute-done.3
  48.6 0.7 constant_dynamic-update-slice_fusion.8
  53.9 0.7 constant_dynamic-update-slice_fusion
  54.5 2.2 %fusion.23 = bf16[128,256]{0,1:T(8,128)(2,1)} fusion(bf16[512,1792]{1,0:T(8,128)(2,1)} %constant_dynamic-update-slice_fusion, s32[]{:T(128)S(6)} %select_n.44, bf16[1,128,1792]{2,1,0:T(8,128)(2,1)S(1)} %copy-done), kind=kOutput, calls=%fused_computation.40 | convolution fusion | flops 117473280 | bytes 1441796 | tf_op jit(solution)/shard_map/dot_general | solution.py:131
  56.8 5.9 %reduce-scatter.3.cloned.1.call-done = bf16[128,128]{0,1:T(8,128)(2,1)} async-done(((bf16[128,256]{0,1:T(8,128)(2,1)}), bf16[128,128]{0,1:T(8,128)(2,1)}) %reduce-scatter.3.cloned.1.call-update) | async-done | bytes 32784 | tf_op jit(solution)/shard_map/reduce_scatter | solution.py:132
  62.8 0.7 slice_convert_fusion
  64.2 0.7 convert_element_type.193
  64.9 4.3 %collective-permute-start.7 = (bf16[28,4096]{1,0:T(8,128)(2,1)}, bf16[28,4096]{1,0:T(8,128)(2,1)}, u32[]{:S(2)}, u32[]{:S(2)}) collective-permute-start(bf16[28,4096]{1,0:T(8,128)(2,1)} %convert_element_type.193), channel_id=1, source_target_pairs={{0,2},{2,4},{4,6},{6,8},{8,10},{10,12},{12,14},{1,3},{3,5},{5,7},{... | collective-permute-start | bytes 688136 | tf_op jit(solution)/shard_map/ppermute | solution.py:25
  69.3 1.5 convolution_bitcast_fusion
  70.8 1.5 copy.71
  72.6 1.3 collective-permute-start.13
  73.9 0.9 collective-permute-done.7
  74.9 1.1 fusion.57
  76.0 5.3 %collective-permute-start.10 = (bf16[28,4096]{1,0:T(8,128)(2,1)S(1)}, bf16[28,4096]{1,0:T(8,128)(2,1)S(1)}, u32[]{:S(2)}, u32[]{:S(2)}) collective-permute-start(bf16[28,4096]{1,0:T(8,128)(2,1)S(1)} %fusion.57), channel_id=1, source_target_pairs={{0,4},{2,6},{4,8},{6,10},{8,12},{10,14},{1,5},{3,7},{5,9},{7,11},{... | collective-permute-start | bytes 688136 | tf_op jit(solution)/shard_map/ppermute | solution.py:25
  81.3 1.3 collective-permute-start.14
  82.6 4.5 %collective-permute-start.9 = (f32[28]{0:T(128)S(1)}, f32[28]{0:T(128)S(1)}, u32[]{:S(2)}, u32[]{:S(2)}) collective-permute-start(f32[28]{0:T(128)S(1)} %exponential_multiply_fusion.1), channel_id=1, source_target_pairs={{0,2},{2,4},{4,6},{6,8},{8,10},{10,12},{12,14},{1,3},{3,5},{5,7},{... | collective-permute-start | bytes 344 | tf_op jit(solution)/shard_map/ppermute | solution.py:25
  87.2 1.3 collective-permute-done.9
  88.5 1.9 fusion.42
  90.4 1.3 collective-permute-start.15
  91.7 0.7 broadcast_compare_fusion
  92.4 7.8 %collective-permute-start.12 = (bf16[28,4096]{1,0:T(8,128)(2,1)}, bf16[28,4096]{1,0:T(8,128)(2,1)}, u32[]{:S(2)}, u32[]{:S(2)}) collective-permute-start(bf16[28,4096]{1,0:T(8,128)(2,1)} %get-tuple-element.40), channel_id=1, source_target_pairs={{0,8},{2,10},{4,12},{6,14},{1,9},{3,11},{5,13},{7,15},{16,24},{18,... | collective-permute-start | bytes 688136 | tf_op jit(solution)/shard_map/ppermute | solution.py:25
  100.2 0.9 fusion.46
  101.1 1.3 collective-permute-start.17
  102.9 0.7 reshape_squeeze.10
  104.0 3.5 %collective-permute-start.11 = (f32[28]{0:T(128)S(1)}, f32[28]{0:T(128)S(1)}, u32[]{:S(2)}, u32[]{:S(2)}) collective-permute-start(f32[28]{0:T(128)S(1)} %get-tuple-element.42), channel_id=1, source_target_pairs={{0,4},{2,6},{4,8},{6,10},{8,12},{10,14},{1,5},{3,7},{5,9},{7,11},{... | collective-permute-start | bytes 344 | tf_op jit(solution)/shard_map/ppermute | solution.py:25
  108.1 1.3 collective-permute-start.16
  109.4 5.4 %collective-permute-done.16 = f32[28]{0:T(128)S(1)} collective-permute-done((f32[28]{0:T(128)S(1)}, f32[28]{0:T(128)S(1)}, u32[]{:S(2)}, u32[]{:S(2)}) %collective-permute-start.16) | collective-permute-done | bytes 144 | tf_op jit(solution)/shard_map/ppermute | solution.py:25
  114.8 0.8 fusion.84
  115.7 3.0 %multiply_reduce_fusion.2 = (f32[28]{0:T(128)}, bf16[28,4096]{1,0:T(8,128)(2,1)S(1)}, f32[28,4096]{1,0:T(8,128)}) fusion(bf16[28,4096]{1,0:T(8,128)(2,1)} %collective-permute-done.17, f32[28]{0:T(128)S(1)} %mul.369, bf16[28,4096]{1,0:T(8,128)(2,1)S(1)} %collective-permute-done.15, f32[28]{0:T(128)} %copy-done.31, ...), kind=kLoop, calls=%fused_computation.80 | loop fusion | flops 1949668 | bytes 2064944 | tf_op jit(solution)/shard_map/reduce_sum | solution.py:181
  118.6 1.4 reshape.211
  120.0 1.3 copy.68
  121.3 1.7 fusion.88
  123.1 0.7 fusion.28
  123.8 1.2 reshape.213
  125.0 1.9 multiply_reduce_fusion
  127.1 1.5 fusion.103
  128.6 0.7 copy.63
  129.2 3.4 %fusion.12 = (f32[28,128]{1,0:T(8,128)}, f32[28,128]{1,0:T(8,128)}, f32[28,128]{1,0:T(8,128)S(1)}, bf16[128,128]{1,0:T(8,128)(2,1)S(1)}) fusion(f32[28,128]{1,0:T(8,128)} %copy.63, f32[128,128]{1,0:T(8,128)} %fusion.84, f32[128,128]{1,0:T(8,128)} %get-tuple-element.46, f32[28,128]{1,0:T(8,128)} %bitcast.236, pred[128,128]{1,0:T(8,128)(4,1)} %get-tuple-element.45, ...), kind=kOutput, calls=%fused_computation.19 | convolution fusion | flops 66491904 | bytes 1169408 | tf_op jit(solution)/shard_map/transpose(jvp(hts,shp->thp))/dot_general | solution.py:29
  132.7 0.7 copy.64
  133.5 1.0 fusion.25
  134.9 2.2 %all_gather.3 = bf16[128,256]{0,1:T(8,128)(2,1)S(1)} all-gather(bf16[128,128]{0,1:T(8,128)(2,1)S(1)} %add_convert_fusion), channel_id=1, replica_groups=mesh['section'=2,'seq'=8,'head'=2] {'head'}, dimensions={1}, use_global_device_ids=true | all-gather | bytes 98304 | tf_op jit(solution)/shard_map/all_gather | solution.py:186
  137.0 1.3 convolution_convert_fusion
  139.5 0.9 fusion.22
  141.3 1.5 fusion.1
  142.8 1.3 collective-permute-start.18
  144.1 0.8 fusion.106
  144.9 0.8 fusion.107
  145.9 20.8 %all-reduce.4 = (f32[1,1792]{1,0:T(1,128)}, f32[1,28]{1,0:T(1,128)}, f32[1,28]{1,0:T(1,128)}, f32[1,28]{1,0:T(1,128)}) all-reduce(f32[1,1792]{1,0:T(1,128)S(1)} %broadcast_in_dim.47, f32[1,28]{1,0:T(1,128)S(1)} %get-tuple-element.50, f32[1,28]{1,0:T(1,128)S(1)} %get-tuple-element.49, ...), channel_id=1, replica_groups=mesh['section'=2,'seq'=8,'head'=2] {'seq'}, use_global_device_ids=true, to_apply=%region_11.13 | all-reduce | flops 1876 | bytes 15008 | tf_op jit(solution)/shard_map/psum | solution.py:201
  166.7 34.3 %reduce-scatter.5.cloned.1.call-done = bf16[32,1792]{1,0:T(8,128)(2,1)} async-done(((bf16[256,1792]{1,0:T(8,128)(2,1)}), bf16[32,1792]{1,0:T(8,128)(2,1)}) %reduce-scatter.5.cloned.1.call-update) | async-done | bytes 114704 | tf_op jit(solution)/shard_map/reduce_scatter | solution.py:193
  201.1 1.6 bitcast_convert_fusion
  202.7 0.8 copy.109
  (156 shorter events, 15.7 us)
Async XLA Ops:
  7.2 13.0 %copy-start.24 = (s32[1,128]{1,0:T(1,128)S(1)}, s32[1,128]{1,0:T(1,128)}, u32[]{:S(2)}) copy-start(s32[1,128]{1,0:T(1,128)} %param.10) | copy-start | bytes 1540
  7.2 12.7 %copy-start.4 = (bf16[1,128,1792]{2,1,0:T(8,128)(2,1)S(1)}, bf16[1,128,1792]{2,1,0:T(8,128)(2,1)}, u32[]{:S(2)}) copy-start(bf16[1,128,1792]{2,1,0:T(8,128)(2,1)} %param.11) | copy-start | bytes 1376260
  7.2 15.8 %copy-start.25 = (f32[1,28]{1,0:T(1,128)S(1)}, f32[1,28]{1,0:T(1,128)}, u32[]{:S(2)}) copy-start(f32[1,28]{1,0:T(1,128)} %param.14) | copy-start | bytes 340
  7.2 55.6 %reduce-scatter.3.cloned.1.call-start = ((), (), s32[]{:S(2)}) async-start(), calls=%async_computation.2 | async-start | bytes 98304 | tf_op jit(solution)/shard_map/reduce_scatter | solution.py:132
  7.2 14.2 %collective-permute-start = (bf16[32,1792]{1,0:T(8,128)(2,1)}, bf16[32,1792]{1,0:T(8,128)(2,1)S(1)}, u32[]{:S(2)}, u32[]{:S(2)}) collective-permute-start(bf16[32,1792]{1,0:T(8,128)(2,1)} %bitcast.230), channel_id=1, source_target_pairs={{0,2},{2,4},{4,6},{6,8},{8,10},{10,12},{12,14},{14,0},{1,3},{3,5},... | collective-permute-start | bytes 344072 | tf_op jit(solution)/shard_map/ppermute | solution.py:15
  10.3 18.8 %collective-permute-start.4 = (bf16[32,1792]{1,0:T(8,128)(2,1)}, bf16[32,1792]{1,0:T(8,128)(2,1)S(1)}, u32[]{:S(2)}, u32[]{:S(2)}) collective-permute-start(bf16[32,1792]{1,0:T(8,128)(2,1)} %bitcast.231), channel_id=1, source_target_pairs={{0,14},{2,0},{4,2},{6,4},{8,6},{10,8},{12,10},{14,12},{1,15},{3,1}... | collective-permute-start | bytes 344072 | tf_op jit(solution)/shard_map/ppermute | solution.py:17
  14.6 5.5 %collective-permute-start.8 = (s32[1]{0:T(128)}, s32[1]{0:T(128)}, u32[]{:S(2)}, u32[]{:S(2)}) collective-permute-start(s32[1]{0:T(128)} %bitcast.19), channel_id=1, source_target_pairs={{0,2},{2,4},{4,6},{6,8},{8,10},{10,12},{12,14},{1,3},{3,5},{5,7},{... | collective-permute-start | bytes 20 | tf_op jit(solution)/shard_map/ppermute | solution.py:25
  16.5 30.2 %copy-start.5 = (bf16[1,32,1792]{2,1,0:T(8,128)(2,1)S(1)}, bf16[1,32,1792]{2,1,0:T(8,128)(2,1)}, u32[]{:S(2)}) copy-start(bf16[1,32,1792]{2,1,0:T(8,128)(2,1)} %param.12) | copy-start | bytes 344068
  19.1 18.8 %copy-start.2 = (f32[28,1,128]{0,2,1:T(8,128)}, f32[28,1,128]{0,2,1:T(8,128)S(1)}, u32[]{:S(2)}) copy-start(f32[28,1,128]{0,2,1:T(8,128)S(1)} %copy.83) | copy-start | bytes 43012
  19.8 9.2 %copy-start.38 = (f32[28]{0:T(128)}, f32[28]{0:T(128)S(1)}, u32[]{:S(2)}) copy-start(f32[28]{0:T(128)S(1)} %negate_bitcast_fusion) | copy-start | bytes 340
  21.4 16.5 %copy-start.35 = (f32[128]{0:T(128)}, f32[128]{0:T(128)S(1)}, u32[]{:S(2)}) copy-start(f32[128]{0:T(128)S(1)} %get-tuple-element.44) | copy-start | bytes 1540
  21.4 31.8 %copy-start.20 = (pred[128]{0:T(512)(128)(4,1)}, pred[128]{0:T(512)(128)(4,1)S(1)}, u32[]{:S(2)}) copy-start(pred[128]{0:T(512)(128)(4,1)S(1)} %get-tuple-element.31) | copy-start | bytes 388
  21.4 31.8 %copy-start.22 = (f32[128]{0:T(128)}, f32[128]{0:T(128)S(1)}, u32[]{:S(2)}) copy-start(f32[128]{0:T(128)S(1)} %get-tuple-element.32) | copy-start | bytes 1540
  21.5 7.5 %collective-permute-start.1 = (bf16[32,1792]{1,0:T(8,128)(2,1)S(1)}, bf16[32,1792]{1,0:T(8,128)(2,1)S(1)}, u32[]{:S(2)}, u32[]{:S(2)}) collective-permute-start(bf16[32,1792]{1,0:T(8,128)(2,1)S(1)} %collective-permute-done), channel_id=1, source_target_pairs={{0,2},{2,4},{4,6},{6,8},{8,10},{10,12},{12,14},{14,0},{1,3},{3,5},... | collective-permute-start | bytes 344072 | tf_op jit(solution)/shard_map/ppermute | solution.py:15
  23.2 30.7 %copy-start.15 = (f32[128,28]{0,1:T(8,128)}, f32[128,28]{0,1:T(8,128)S(1)}, u32[]{:S(2)}) copy-start(f32[128,28]{0,1:T(8,128)S(1)} %get-tuple-element.48) | copy-start | bytes 43012
  29.0 7.5 %collective-permute-start.2 = (bf16[32,1792]{1,0:T(8,128)(2,1)S(1)}, bf16[32,1792]{1,0:T(8,128)(2,1)S(1)}, u32[]{:S(2)}, u32[]{:S(2)}) collective-permute-start(bf16[32,1792]{1,0:T(8,128)(2,1)S(1)} %collective-permute-done.1), channel_id=1, source_target_pairs={{0,2},{2,4},{4,6},{6,8},{8,10},{10,12},{12,14},{14,0},{1,3},{3,5},... | collective-permute-start | bytes 344072 | tf_op jit(solution)/shard_map/ppermute | solution.py:15
  29.0 24.8 %copy-start.27 = (f32[28]{0:T(128)}, f32[28]{0:T(128)S(1)}, u32[]{:S(2)}) copy-start(f32[28]{0:T(128)S(1)} %slice_bitcast_fusion) | copy-start | bytes 340
  29.0 8.9 %collective-permute-start.5 = (bf16[32,1792]{1,0:T(8,128)(2,1)S(1)}, bf16[32,1792]{1,0:T(8,128)(2,1)S(1)}, u32[]{:S(2)}, u32[]{:S(2)}) collective-permute-start(bf16[32,1792]{1,0:T(8,128)(2,1)S(1)} %collective-permute-done.4), channel_id=1, source_target_pairs={{0,14},{2,0},{4,2},{6,4},{8,6},{10,8},{12,10},{14,12},{1,15},{3,1}... | collective-permute-start | bytes 344072 | tf_op jit(solution)/shard_map/ppermute | solution.py:17
  36.5 7.6 %collective-permute-start.3 = (bf16[32,1792]{1,0:T(8,128)(2,1)S(1)}, bf16[32,1792]{1,0:T(8,128)(2,1)S(1)}, u32[]{:S(2)}, u32[]{:S(2)}) collective-permute-start(bf16[32,1792]{1,0:T(8,128)(2,1)S(1)} %collective-permute-done.2), channel_id=1, source_target_pairs={{0,2},{2,4},{4,6},{6,8},{8,10},{10,12},{12,14},{14,0},{1,3},{3,5},... | collective-permute-start | bytes 344072 | tf_op jit(solution)/shard_map/ppermute | solution.py:15
  38.0 16.6 %copy-start = (bf16[1,128,1792]{2,1,0:T(8,128)(2,1)S(1)}, bf16[1,128,1792]{2,1,0:T(8,128)(2,1)}, u32[]{:S(2)}) copy-start(bf16[1,128,1792]{2,1,0:T(8,128)(2,1)} %param.9) | copy-start | bytes 1376260
  38.0 10.6 %collective-permute-start.6 = (bf16[32,1792]{1,0:T(8,128)(2,1)S(1)}, bf16[32,1792]{1,0:T(8,128)(2,1)S(1)}, u32[]{:S(2)}, u32[]{:S(2)}) collective-permute-start(bf16[32,1792]{1,0:T(8,128)(2,1)S(1)} %collective-permute-done.5), channel_id=1, source_target_pairs={{0,14},{2,0},{4,2},{6,4},{8,6},{10,8},{12,10},{14,12},{1,15},{3,1}... | collective-permute-start | bytes 344072 | tf_op jit(solution)/shard_map/ppermute | solution.py:17
  56.8 144.3 %reduce-scatter.5.cloned.1.call-start = ((), (), s32[]{:S(2)}) async-start(), calls=%async_computation.3 | async-start | bytes 1032192 | tf_op jit(solution)/shard_map/reduce_scatter | solution.py:193
  63.5 7.3 %copy-start.8 = (f32[128,64]{0,1:T(8,128)}, f32[128,64]{0,1:T(8,128)S(1)}, u32[]{:S(2)}) copy-start(f32[128,64]{0,1:T(8,128)S(1)} %slice_convert_fusion) | copy-start | bytes 98308
  63.5 5.8 %copy-start.6 = (bf16[128,128]{0,1:T(8,128)(2,1)S(1)}, bf16[128,128]{0,1:T(8,128)(2,1)}, u32[]{:S(2)}) copy-start(bf16[128,128]{0,1:T(8,128)(2,1)} %reduce-scatter.3.cloned.1.call-done) | copy-start | bytes 98308
  64.9 10.0 %collective-permute-start.7 = (bf16[28,4096]{1,0:T(8,128)(2,1)}, bf16[28,4096]{1,0:T(8,128)(2,1)}, u32[]{:S(2)}, u32[]{:S(2)}) collective-permute-start(bf16[28,4096]{1,0:T(8,128)(2,1)} %convert_element_type.193), channel_id=1, source_target_pairs={{0,2},{2,4},{4,6},{6,8},{8,10},{10,12},{12,14},{1,3},{3,5},{5,7},{... | collective-permute-start | bytes 688136 | tf_op jit(solution)/shard_map/ppermute | solution.py:25
  72.6 15.8 %collective-permute-start.13 = (bf16[28,4096]{1,0:T(8,128)(2,1)S(1)}, bf16[28,4096]{1,0:T(8,128)(2,1)S(1)}, u32[]{:S(2)}, u32[]{:S(2)}) collective-permute-start(bf16[28,4096]{1,0:T(8,128)(2,1)S(1)} %convert_element_type.204), channel_id=1, source_target_pairs={{2,0},{4,2},{6,4},{8,6},{10,8},{12,10},{14,12},{3,1},{5,3},{7,5},{... | collective-permute-start | bytes 688136 | tf_op jit(solution)/shard_map/ppermute | solution.py:25
  76.0 12.5 %collective-permute-start.10 = (bf16[28,4096]{1,0:T(8,128)(2,1)S(1)}, bf16[28,4096]{1,0:T(8,128)(2,1)S(1)}, u32[]{:S(2)}, u32[]{:S(2)}) collective-permute-start(bf16[28,4096]{1,0:T(8,128)(2,1)S(1)} %fusion.57), channel_id=1, source_target_pairs={{0,4},{2,6},{4,8},{6,10},{8,12},{10,14},{1,5},{3,7},{5,9},{7,11},{... | collective-permute-start | bytes 688136 | tf_op jit(solution)/shard_map/ppermute | solution.py:25
  81.3 5.9 %collective-permute-start.14 = (f32[28]{0:T(128)S(1)}, f32[28]{0:T(128)S(1)}, u32[]{:S(2)}, u32[]{:S(2)}) collective-permute-start(f32[28]{0:T(128)S(1)} %exponential_multiply_fusion.1), channel_id=1, source_target_pairs={{2,0},{4,2},{6,4},{8,6},{10,8},{12,10},{14,12},{3,1},{5,3},{7,5},{... | collective-permute-start | bytes 344 | tf_op jit(solution)/shard_map/ppermute | solution.py:25
  82.6 5.8 %collective-permute-start.9 = (f32[28]{0:T(128)S(1)}, f32[28]{0:T(128)S(1)}, u32[]{:S(2)}, u32[]{:S(2)}) collective-permute-start(f32[28]{0:T(128)S(1)} %exponential_multiply_fusion.1), channel_id=1, source_target_pairs={{0,2},{2,4},{4,6},{6,8},{8,10},{10,12},{12,14},{1,3},{3,5},{5,7},{... | collective-permute-start | bytes 344 | tf_op jit(solution)/shard_map/ppermute | solution.py:25
  87.2 27.6 %copy-start.31 = (f32[28]{0:T(128)}, f32[28]{0:T(128)S(1)}, u32[]{:S(2)}) copy-start(f32[28]{0:T(128)S(1)} %collective-permute-done.14) | copy-start | bytes 340
  88.5 21.0 %copy-start.32 = (f32[28]{0:T(128)}, f32[28]{0:T(128)S(1)}, u32[]{:S(2)}) copy-start(f32[28]{0:T(128)S(1)} %collective-permute-done.9) | copy-start | bytes 340
  88.5 13.9 %copy-start.37 = (f32[1,28]{1,0:T(1,128)S(1)}, f32[1,28]{1,0:T(1,128)}, u32[]{:S(2)}) copy-start(f32[1,28]{1,0:T(1,128)} %param.16) | copy-start | bytes 340
  90.4 9.8 %collective-permute-start.15 = (bf16[28,4096]{1,0:T(8,128)(2,1)S(1)}, bf16[28,4096]{1,0:T(8,128)(2,1)S(1)}, u32[]{:S(2)}, u32[]{:S(2)}) collective-permute-start(bf16[28,4096]{1,0:T(8,128)(2,1)S(1)} %get-tuple-element.41), channel_id=1, source_target_pairs={{4,0},{6,2},{8,4},{10,6},{12,8},{14,10},{5,1},{7,3},{9,5},{11,7},{... | collective-permute-start | bytes 688136 | tf_op jit(solution)/shard_map/ppermute | solution.py:25
  92.4 23.3 %collective-permute-start.12 = (bf16[28,4096]{1,0:T(8,128)(2,1)}, bf16[28,4096]{1,0:T(8,128)(2,1)}, u32[]{:S(2)}, u32[]{:S(2)}) collective-permute-start(bf16[28,4096]{1,0:T(8,128)(2,1)} %get-tuple-element.40), channel_id=1, source_target_pairs={{0,8},{2,10},{4,12},{6,14},{1,9},{3,11},{5,13},{7,15},{16,24},{18,... | collective-permute-start | bytes 688136 | tf_op jit(solution)/shard_map/ppermute | solution.py:25
  101.1 14.5 %collective-permute-start.17 = (bf16[28,4096]{1,0:T(8,128)(2,1)}, bf16[28,4096]{1,0:T(8,128)(2,1)}, u32[]{:S(2)}, u32[]{:S(2)}) collective-permute-start(bf16[28,4096]{1,0:T(8,128)(2,1)} %fusion.46), channel_id=1, source_target_pairs={{8,0},{10,2},{12,4},{14,6},{9,1},{11,3},{13,5},{15,7},{24,16},{26,... | collective-permute-start | bytes 688136 | tf_op jit(solution)/shard_map/ppermute | solution.py:25
  104.0 5.4 %collective-permute-start.11 = (f32[28]{0:T(128)S(1)}, f32[28]{0:T(128)S(1)}, u32[]{:S(2)}, u32[]{:S(2)}) collective-permute-start(f32[28]{0:T(128)S(1)} %get-tuple-element.42), channel_id=1, source_target_pairs={{0,4},{2,6},{4,8},{6,10},{8,12},{10,14},{1,5},{3,7},{5,9},{7,11},{... | collective-permute-start | bytes 344 | tf_op jit(solution)/shard_map/ppermute | solution.py:25
  108.1 6.7 %collective-permute-start.16 = (f32[28]{0:T(128)S(1)}, f32[28]{0:T(128)S(1)}, u32[]{:S(2)}, u32[]{:S(2)}) collective-permute-start(f32[28]{0:T(128)S(1)} %get-tuple-element.43), channel_id=1, source_target_pairs={{4,0},{6,2},{8,4},{10,6},{12,8},{14,10},{5,1},{7,3},{9,5},{11,7},{... | collective-permute-start | bytes 344 | tf_op jit(solution)/shard_map/ppermute | solution.py:25
  129.2 4.2 %copy-start.7 = (bf16[128,128]{0,1:T(8,128)(2,1)S(1)}, bf16[128,128]{0,1:T(8,128)(2,1)}, u32[]{:S(2)}) copy-start(bf16[128,128]{0,1:T(8,128)(2,1)} %reduce-scatter.3.cloned.1.call-done) | copy-start | bytes 98308
  132.7 2.2 %copy-start.18 = (bf16[128,64]{0,1:T(8,128)(2,1)S(1)}, bf16[128,64]{0,1:T(8,128)(2,1)}, u32[]{:S(2)}) copy-start(bf16[128,64]{0,1:T(8,128)(2,1)} %get-tuple-element.14) | copy-start | bytes 49156
  133.5 4.9 %copy-start.29 = (f32[28]{0:T(128)S(1)}, f32[28]{0:T(128)}, u32[]{:S(2)}) copy-start(f32[28]{0:T(128)} %get-tuple-element.26) | copy-start | bytes 340
  133.5 4.9 %copy-start.30 = (f32[28]{0:T(128)S(1)}, f32[28]{0:T(128)}, u32[]{:S(2)}) copy-start(f32[28]{0:T(128)} %get-tuple-element.29) | copy-start | bytes 340
  134.6 4.1 %copy-start.3 = (f32[28,1,128]{0,2,1:T(8,128)S(1)}, f32[28,1,128]{0,2,1:T(8,128)}, u32[]{:S(2)}) copy-start(f32[28,1,128]{0,2,1:T(8,128)} %copy-done.2) | copy-start | bytes 43012
  134.6 4.1 %copy-start.11 = (f32[28,128]{0,1:T(8,128)S(1)}, f32[28,128]{0,1:T(8,128)}, u32[]{:S(2)}) copy-start(f32[28,128]{0,1:T(8,128)} %copy.64) | copy-start | bytes 43012
  134.6 4.1 %copy-start.14 = (f32[128,28]{0,1:T(8,128)S(1)}, f32[128,28]{0,1:T(8,128)}, u32[]{:S(2)}) copy-start(f32[128,28]{0,1:T(8,128)} %fusion.28) | copy-start | bytes 43012
  134.6 4.1 %copy-start.16 = (f32[128,28]{0,1:T(8,128)S(1)}, f32[128,28]{0,1:T(8,128)}, u32[]{:S(2)}) copy-start(f32[128,28]{0,1:T(8,128)} %copy-done.15) | copy-start | bytes 43012
  134.6 4.1 %copy-start.21 = (pred[128]{0:T(512)(128)(4,1)S(1)}, pred[128]{0:T(512)(128)(4,1)}, u32[]{:S(2)}) copy-start(pred[128]{0:T(512)(128)(4,1)} %copy-done.20) | copy-start | bytes 388
  134.6 4.1 %copy-start.23 = (f32[128]{0:T(128)S(1)}, f32[128]{0:T(128)}, u32[]{:S(2)}) copy-start(f32[128]{0:T(128)} %copy-done.22) | copy-start | bytes 1540
  134.6 4.1 %copy-start.26 = (f32[1,28]{1,0:T(1,128)S(1)}, f32[1,28]{1,0:T(1,128)}, u32[]{:S(2)}) copy-start(f32[1,28]{1,0:T(1,128)} %param.14) | copy-start | bytes 340
  134.6 4.1 %copy-start.28 = (f32[28]{0:T(128)S(1)}, f32[28]{0:T(128)}, u32[]{:S(2)}) copy-start(f32[28]{0:T(128)} %copy-done.27) | copy-start | bytes 340
  134.6 4.1 %copy-start.36 = (f32[128]{0:T(128)S(1)}, f32[128]{0:T(128)}, u32[]{:S(2)}) copy-start(f32[128]{0:T(128)} %copy-done.35) | copy-start | bytes 1540
  134.6 4.1 %copy-start.39 = (f32[28]{0:T(128)S(1)}, f32[28]{0:T(128)}, u32[]{:S(2)}) copy-start(f32[28]{0:T(128)} %copy-done.38) | copy-start | bytes 340
  134.7 4.1 %copy-start.41 = (f32[28,128]{1,0:T(8,128)S(1)}, f32[28,128]{1,0:T(8,128)}, u32[]{:S(2)}) copy-start(f32[28,128]{1,0:T(8,128)} %get-tuple-element.10) | copy-start | bytes 43012
  134.7 4.1 %copy-start.42 = (f32[28,128]{1,0:T(8,128)S(1)}, f32[28,128]{1,0:T(8,128)}, u32[]{:S(2)}) copy-start(f32[28,128]{1,0:T(8,128)} %get-tuple-element.11) | copy-start | bytes 43012
  134.8 4.6 %copy-start.10 = (f32[28,64]{1,0:T(8,128)S(1)}, f32[28,64]{1,0:T(8,128)}, u32[]{:S(2)}) copy-start(f32[28,64]{1,0:T(8,128)} %reshape_squeeze.10) | copy-start | bytes 21508
  134.8 4.6 %copy-start.12 = (f32[128,128]{1,0:T(8,128)S(1)}, f32[128,128]{1,0:T(8,128)}, u32[]{:S(2)}) copy-start(f32[128,128]{1,0:T(8,128)} %fusion.84) | copy-start | bytes 196612
  134.8 4.6 %copy-start.13 = (f32[128,128]{1,0:T(8,128)S(1)}, f32[128,128]{1,0:T(8,128)}, u32[]{:S(2)}) copy-start(f32[128,128]{1,0:T(8,128)} %get-tuple-element.46) | copy-start | bytes 196612
  134.8 4.6 %copy-start.17 = (f32[28,128]{1,0:T(8,128)S(1)}, f32[28,128]{1,0:T(8,128)}, u32[]{:S(2)}) copy-start(f32[28,128]{1,0:T(8,128)} %copy.63) | copy-start | bytes 43012
  134.8 4.6 %copy-start.19 = (pred[128,128]{1,0:T(8,128)(4,1)S(1)}, pred[128,128]{1,0:T(8,128)(4,1)}, u32[]{:S(2)}) copy-start(pred[128,128]{1,0:T(8,128)(4,1)} %get-tuple-element.45) | copy-start | bytes 49156
  134.8 4.6 %copy-start.40 = (f32[28]{0:T(128)S(1)}, f32[28]{0:T(128)}, u32[]{:S(2)}) copy-start(f32[28]{0:T(128)} %add_bitcast_fusion.1) | copy-start | bytes 340
  139.5 1.0 copy-start.1
  139.5 1.0 copy-start.9
  141.3 4.6 %copy-start.34 = (f32[1,28]{1,0:T(1,128)S(1)}, f32[1,28]{1,0:T(1,128)}, u32[]{:S(2)}) copy-start(f32[1,28]{1,0:T(1,128)} %param.15) | copy-start | bytes 340
  141.3 4.6 %copy-start.33 = (f32[28]{0:T(128)S(1)}, f32[28]{0:T(128)}, u32[]{:S(2)}) copy-start(f32[28]{0:T(128)} %reduce_sum.161) | copy-start | bytes 340
  142.8 23.9 %collective-permute-start.18 = (bf16[1,128,1792]{2,1,0:T(8,128)(2,1)S(1)}, bf16[1,128,1792]{2,1,0:T(8,128)(2,1)S(1)}, u32[]{:S(2)}, u32[]{:S(2)}) collective-permute-start(bf16[1,128,1792]{2,1,0:T(8,128)(2,1)S(1)} %fusion.1), channel_id=1, source_target_pairs={{16,0},{17,1},{18,2},{19,3},{20,4},{21,5},{22,6},{23,7},{24,8},{25... | collective-permute-start | bytes 1376264 | tf_op jit(solution)/shard_map/ppermute | solution.py:25
Sparse Core Ops, SparseCore 0:
  56.9 5.8 reduce-scatter.2
  138.5 62.4 reduce-scatter.4
